TPU v7x, 128 devices: a whole 4x4x4 slice. The times are simulated.
128 devices in a mesh: req: 16 (over y, z), mlp: 8 (over x, core).
Axes of the slice: x: 4, y: 4, z: 4, core: 2. Of those that a mesh axis runs over, the one named last changes fastest.
Arguments:
- resid: bfloat16 [2176, 5120], P('req', 'mlp'), may hold values from -180 to 180
- queries: bfloat16 [2176, 5120], P('req', 'mlp'), may hold values from -200 to 200
- new_keys: bfloat16 [2176, 1024], P('req', 'mlp'), may hold values from -6 to 6
- new_values: bfloat16 [2176, 1024], P('req', 'mlp'), may hold values from -6 to 6
- cache_keys: bfloat16 [48, 4096, 1024], P('req', None, 'mlp'), may hold values from -6 to 6
- cache_values: bfloat16 [48, 4096, 1024], P('req', None, 'mlp'), may hold values from -6 to 6
- context_keys: bfloat16 [5, 1024, 1024], P(None, 'req', 'mlp'), may hold values from -6 to 6
- context_values: bfloat16 [5, 1024, 1024], P(None, 'req', 'mlp'), may hold values from -6 to 6
- cache_lengths: int32 [48], P('req'), may hold values from 1 to 4096, 49152 in all
- group_ids: int32 [48], P('req'), may hold values from 0 to 3
- prefix_lengths: int32 [4], replicated, may hold values from 1 to 1024, 2048 in all
- prompt_start: int32 [1], replicated, may hold values from 1 to 1023
- out_weight: bfloat16 [5120, 5120], P('mlp'), may hold values from -1.25 to 1.25
- norm_gain: float32 [5120], P('mlp'), may hold values from 0.5 to 1.5
- gate_weight: bfloat16 [5120, 27648], P(None, ('req', 'mlp')), may hold values from -0.078125 to 0.078125
- up_weight: bfloat16 [5120, 27648], P(None, ('req', 'mlp')), may hold values from -0.078125 to 0.078125
- down_weight: bfloat16 [27648, 5120], P('req', 'mlp'), may hold values from -0.109375 to 0.109375
Outputs:
- out: bfloat16 [2176, 5120], P('req', 'mlp')
Inputs may be any that keep to these rules, and one draw needn't show every extreme that they name: `cache_lengths`: one decode request has 4096 valid positions. `prefix_lengths`: one group's prompt has 1024 positions.
All inputs are finite; a program needn't handle non-finite values. No bound on the sum of `cache_lengths` on one device may be relied on, other than what follows from the above.
Results may differ from a plain program's by a relative error of at most 0.019.
Values may be sent and summed in bfloat16 or wider, within the bound.
No kernel may reach another device: no remote copies, remote signals or barrier semaphores. Data moves between devices by JAX's collectives and lax.ppermute only.
A program may use at most 128 MiB of HBM per device.

v0:
```python
import math
import jax
import jax.numpy as jnp
from jax import lax
from jax.sharding import PartitionSpec as P

D = 5120
HQ = 40
KV = 8
HD = 128
NEGATIVE = -1e30


def absorb(carried, scores, allowed, values, pattern):
    running, totals, summed = carried
    scores = jnp.where(allowed, scores, -jnp.inf)
    highest = jnp.maximum(running, jnp.max(scores, axis=-1))
    exponent = jnp.where(allowed, jnp.exp(scores - highest[..., None]), 0.0)
    fading = jnp.exp(running - highest)
    weights = exponent.astype(jnp.bfloat16)
    summed = summed * fading[..., None] + jnp.einsum(
        pattern, weights, values, preferred_element_type=jnp.float32
    )
    totals = totals * fading + jnp.sum(exponent, axis=-1)
    return (highest, totals, summed)


def per_device(
    resid,
    queries,
    new_keys,
    new_values,
    cache_keys,
    cache_values,
    context_keys,
    context_values,
    cache_lengths,
    group_ids,
    prefix_lengths,
    prompt_start,
    out_weight,
    norm_gain,
    gate_weight,
    up_weight,
    down_weight,
):
    rows_here = queries.shape[0]
    decode_count = cache_keys.shape[0]
    prompt_count = rows_here - decode_count
    heads_kv = new_keys.shape[1] // HD
    group_size = HQ // KV
    scaling = 1.0 / math.sqrt(HD)
    cache_span = cache_keys.shape[1]
    context_count = context_keys.shape[0]
    query_rows = queries.reshape(rows_here, heads_kv, group_size, HD)
    query_decode = query_rows[:decode_count]
    query_prompt = query_rows[decode_count:]
    key_rows = new_keys.reshape(rows_here, heads_kv, HD)
    value_rows = new_values.reshape(rows_here, heads_kv, HD)

    def fresh_state(row_count):
        return (
            jnp.full((row_count, heads_kv, group_size), NEGATIVE, jnp.float32),
            jnp.zeros((row_count, heads_kv, group_size), jnp.float32),
            jnp.zeros((row_count, heads_kv, group_size, HD), jnp.float32),
        )

    past_keys = cache_keys.reshape(decode_count, cache_span, heads_kv, HD)
    past_values = cache_values.reshape(decode_count, cache_span, heads_kv, HD)
    scores = (
        jnp.einsum("ikgd,ickd->ikgc", query_decode, past_keys, preferred_element_type=jnp.float32)
        * scaling
    )
    usable = (jnp.arange(cache_span)[None, :] < cache_lengths[:, None])[:, None, None, :]
    decode_state = absorb(fresh_state(decode_count), scores, usable, past_values, "ikgc,ickd->ikgd")
    own_scores = (
        jnp.einsum(
            "ikgd,ikd->ikg",
            query_decode,
            key_rows[:decode_count],
            preferred_element_type=jnp.float32,
        )[..., None]
        * scaling
    )
    decode_state = absorb(
        decode_state,
        own_scores,
        jnp.ones(own_scores.shape, dtype=bool),
        value_rows[:decode_count][:, None],
        "ikgc,ickd->ikgd",
    )
    prompt_length = prompt_start[0]
    prefix_here = prefix_lengths[group_ids]
    state_decode = decode_state
    state_prompt = fresh_state(prompt_count)
    req_count = lax.axis_size("req")
    context_rows = context_keys.shape[1]
    context_pack = jnp.concatenate(
        [
            context_keys.reshape(context_count * context_rows, heads_kv * HD),
            context_values.reshape(context_count * context_rows, heads_kv * HD),
        ],
        0,
    )
    context_gathered = lax.all_gather(context_pack, "req", axis=0, tiled=False)
    new_pack = jnp.concatenate([new_keys, new_values], 0)
    new_copies = jnp.broadcast_to(new_pack[None], (req_count,) + new_pack.shape)
    new_gathered = lax.all_to_all(
        new_copies.reshape(req_count * new_pack.shape[0], -1), "req", 0, 0, tiled=True
    ).reshape(req_count, new_pack.shape[0], -1)
    context_span = context_count * context_rows

    def context_of(offset):
        piece = context_gathered[:, offset : offset + context_span]
        piece = piece.reshape(req_count, context_count, context_rows, heads_kv * HD)
        return jnp.transpose(piece, (1, 0, 2, 3)).reshape(
            context_count, req_count * context_rows, heads_kv * HD
        )

    def prompt_of(offset):
        piece = new_gathered[:, offset : offset + rows_here][:, decode_count:]
        return piece.reshape(req_count * prompt_count, heads_kv * HD)

    key_block = context_of(0)
    value_block = context_of(context_span)
    extent = key_block.shape[1]
    positions = jnp.arange(extent)
    key_split = key_block.reshape(context_count, extent, heads_kv, HD)
    value_split = value_block.reshape(context_count, extent, heads_kv, HD)
    chosen_keys = key_split[group_ids]
    chosen_values = value_split[group_ids]
    block_scores = (
        jnp.einsum("ikgd,ickd->ikgc", query_decode, chosen_keys, preferred_element_type=jnp.float32)
        * scaling
    )
    block_usable = (positions[None, :] < prefix_here[:, None])[:, None, None, :]
    state_decode = absorb(
        state_decode, block_scores, block_usable, chosen_values, "ikgc,ickd->ikgd"
    )
    block_scores = (
        jnp.einsum(
            "jkgd,ckd->jkgc",
            query_prompt,
            key_split[context_count - 1],
            preferred_element_type=jnp.float32,
        )
        * scaling
    )
    block_usable = (positions < prompt_length)[None, None, None, :]
    state_prompt = absorb(
        state_prompt, block_scores, block_usable, value_split[context_count - 1], "jkgc,ckd->jkgd"
    )
    prompt_state = state_prompt
    own_positions = lax.axis_index("req") * prompt_count + jnp.arange(prompt_count, dtype=jnp.int32)
    key_block = prompt_of(0)
    value_block = prompt_of(rows_here)
    extent = key_block.shape[0]
    positions = jnp.arange(extent, dtype=jnp.int32)
    block_scores = (
        jnp.einsum(
            "jkgd,ckd->jkgc",
            query_prompt,
            key_block.reshape(extent, heads_kv, HD),
            preferred_element_type=jnp.float32,
        )
        * scaling
    )
    block_usable = (positions[None, :] <= own_positions[:, None])[:, None, None, :]
    prompt_state = absorb(
        prompt_state,
        block_scores,
        block_usable,
        value_block.reshape(extent, heads_kv, HD),
        "jkgc,ckd->jkgd",
    )

    def finish(carried):
        return (carried[2] / carried[1][..., None]).astype(jnp.bfloat16)

    attended = jnp.concatenate([finish(state_decode), finish(prompt_state)], 0).reshape(
        rows_here, heads_kv * group_size * HD
    )
    mlp_count = lax.axis_size("mlp")
    head_partial = jnp.dot(attended, out_weight, preferred_element_type=jnp.float32)
    pieces = lax.all_to_all(head_partial.astype(jnp.bfloat16), "mlp", 1, 0, tiled=True)
    projected = jnp.sum(pieces.reshape(mlp_count, rows_here, -1).astype(jnp.float32), axis=0)
    mixed = (resid.astype(jnp.float32) + projected).astype(jnp.bfloat16)
    mixed_wide = mixed.astype(jnp.float32)
    mixed_rows = lax.all_gather(mixed, "mlp", axis=1, tiled=True).astype(jnp.float32)
    square_total = jnp.sum(mixed_rows * mixed_rows, axis=1)
    half = D // 2
    side = lax.axis_index("mlp") % 2
    own_half = lax.dynamic_slice_in_dim(mixed_rows, side * half, half, axis=1)
    own_gain = lax.dynamic_slice_in_dim(norm_gain, side * half, half, axis=0)
    normed = (own_half * lax.rsqrt(square_total / D + 1e-06)[:, None] * own_gain[None, :]).astype(
        jnp.bfloat16
    )
    near_rows = lax.all_gather(normed, "req", axis=0, tiled=True)
    pairs = [(i, i ^ 1) for i in range(mlp_count)]
    far_rows = lax.ppermute(near_rows, "mlp", pairs)

    def project(weight):
        near_weight = lax.dynamic_slice_in_dim(weight, side * half, half, axis=0)
        far_weight = lax.dynamic_slice_in_dim(weight, (1 - side) * half, half, axis=0)
        return jnp.dot(near_rows, near_weight, preferred_element_type=jnp.float32) + jnp.dot(
            far_rows, far_weight, preferred_element_type=jnp.float32
        )

    width = gate_weight.shape[1]
    both_proj = project(jnp.concatenate([gate_weight, up_weight], 1))
    gate_proj = both_proj[:, :width]
    up_proj = both_proj[:, width:]
    hidden = (jax.nn.silu(gate_proj) * up_proj).astype(jnp.bfloat16)
    hidden_block = lax.all_gather(hidden, "mlp", axis=1, tiled=True)
    down_partial = jnp.dot(hidden_block, down_weight, preferred_element_type=jnp.float32)
    req_pieces = lax.all_to_all(down_partial.astype(jnp.bfloat16), "req", 0, 0, tiled=True)
    feed = jnp.sum(req_pieces.reshape(req_count, rows_here, -1).astype(jnp.float32), axis=0)
    return (mixed_wide + feed).astype(jnp.bfloat16)


def solution(mesh):
    return jax.shard_map(
        per_device,
        mesh=mesh,
        in_specs=(
            P("req", "mlp"),
            P("req", "mlp"),
            P("req", "mlp"),
            P("req", "mlp"),
            P("req", None, "mlp"),
            P("req", None, "mlp"),
            P(None, "req", "mlp"),
            P(None, "req", "mlp"),
            P("req"),
            P("req"),
            P(),
            P(),
            P("mlp", None),
            P(),
            P(None, ("req", "mlp")),
            P(None, ("req", "mlp")),
            P("req", "mlp"),
        ),
        out_specs=P("req", "mlp"),
        check_vma=False,
    )
```

profile of v0, /device:TPU:0, one launch (start us, length us, event | category | flops | bytes accessed | tf_op | source)
XLA Modules:
  0.0 356.5 jit_solution(12019672314609117947)
XLA Ops:
  6.6 1.8 pad_maximum_fusion
  8.4 0.8 pad_maximum_fusion.1
  9.2 1.1 broadcast_in_dim.145
  10.3 8.2 %all-to-all-start = ((bf16[16,272,128]{2,1,0:T(8,128)(2,1)}), bf16[16,272,128]{2,1,0:T(8,128)(2,1)}, u32[]{:S(2)}, u32[]{:S(2)}) async-start(bf16[16,272,128]{2,1,0:T(8,128)(2,1)} %broadcast_in_dim.145), calls=%async_computation | async-start | bytes 2228224 | tf_op jit(solution)/shard_map/all_to_all | solution.py:108
  21.1 0.7 slice_bitcast_fusion
  21.8 1.2 slice_convert_fusion
  23.0 0.7 iota_compare_fusion.2
  25.0 0.9 reshape.390
  25.9 2.2 fusion.91
  28.4 10.5 %all-to-all-done = bf16[16,272,128]{2,1,0:T(8,128)(2,1)} async-done(((bf16[16,272,128]{2,1,0:T(8,128)(2,1)}), bf16[16,272,128]{2,1,0:T(8,128)(2,1)}, u32[]{:S(2)}, u32[]{:S(2)}) %all-to-all-start) | async-done | bytes 1114144 | tf_op jit(solution)/shard_map/all_to_all | solution.py:108
  38.9 1.6 fusion.89
  40.5 1.0 reshape.439
  41.7 3.7 %fusion.90 = (f32[133,5]{0,1:T(8,128)S(1)}, f32[133,1,5,2128]{3,0,2,1:T(8,128)}) fusion(bf16[2128,128,1]{1,0,2:T(8,128)(2,1)S(1)} %reshape.438, bf16[133,5,128]{2,1,0:T(8,128)(2,1)S(1)} %copy-done.5, pred[133,2128]{1,0:T(8,128)(4,1)S(1)} %iota_compare_fusion), kind=kOutput, calls=%fused_computation.124 | convolution fusion | flops 366515392 | bytes 6661172 | tf_op jit(solution)/shard_map/jkgd,ckd->jkgc/dot_general | solution.py:160
  45.4 18.5 %all-gather.14.cloned.1.call-done = bf16[10240,128]{1,0:T(8,128)(2,1)} async-done(((bf16[640,128]{1,0:T(8,128)(2,1)}), bf16[10240,128]{1,0:T(8,128)(2,1)}) %all-gather.14.cloned.1.call-update) | async-done | bytes 2621456 | tf_op jit(solution)/shard_map/all_gather | solution.py:105
  64.0 1.9 fusion.88
  65.9 0.7 slice.67
  66.6 1.3 copy.27
  67.9 0.7 slice.66
  68.6 1.2 copy.26
  69.8 2.1 gather_fusion.2
  71.9 3.0 gather_fusion.1
  75.0 1.6 fusion.92
  77.3 0.9 multiply_add_fusion.1
  78.2 2.5 fusion.45
  80.7 0.7 bitcast_reduce_fusion
  81.5 1.4 fusion
  82.9 0.8 fusion.14
  83.8 0.8 fusion.34
  84.9 1.2 fusion.52
  86.3 0.9 slice-done.3
  87.1 1.3 convolution_convert_fusion
  88.6 23.8 %all_to_all.28 = bf16[136,8,640]{2,0,1:T(8,128)(2,1)S(1)} all-to-all(bf16[136,8,640]{2,0,1:T(8,128)(2,1)S(1)} %bitcast.174), channel_id=1, replica_groups=mesh['req'=16,'mlp'=8] {'mlp'}, dimensions={1} | all-to-all | bytes 2785280 | tf_op jit(solution)/shard_map/all_to_all | solution.py:185
  112.7 0.7 add_convert_fusion.1
  113.5 12.9 %all-gather.2 = f32[8,1,640]{2,1,0:T(1,128)S(1)} all-gather(f32[1,1,640]{2,1,0:T(1,128)S(1)} %reshape.432), channel_id=2, replica_groups=mesh['req'=16,'mlp'=8] {'mlp'}, dimensions={0}, use_global_device_ids=true | all-gather | bytes 23040 | tf_op args[13]
  126.5 8.4 %all-gather.8.cloned.1.call-done = bf16[136,5120]{1,0:T(8,128)(2,1)} async-done(((bf16[136,640]{1,0:T(8,128)(2,1)}), bf16[136,5120]{1,0:T(8,128)(2,1)}) %all-gather.8.cloned.1.call-update) | async-done | bytes 1392656 | tf_op jit(solution)/shard_map/all_gather | solution.py:189
  134.9 1.7 multiply_reduce_fusion
  136.6 1.8 convert_element_type.68
  138.4 1.1 multiply_convert_fusion
  139.6 83.5 %all-gather.10.cloned.1.call-done = bf16[2176,2560]{1,0:T(8,128)(2,1)} async-done(((bf16[136,2560]{1,0:T(8,128)(2,1)}), bf16[2176,2560]{1,0:T(8,128)(2,1)}) %all-gather.10.cloned.1.call-update) | async-done | bytes 11141136 | tf_op jit(solution)/shard_map/all_gather | solution.py:198
  223.2 1.5 copy-done.4
  224.8 8.4 %fusion.12 = f32[2176,432]{0,1:T(8,128)S(1)} fusion(bf16[2176,2560]{1,0:T(8,128)(2,1)} %all-gather.10.cloned.1.call-done, bf16[5120,432]{0,1:T(8,128)(2,1)S(1)} %constant_dynamic-update-slice_fusion, s32[]{:T(128)S(6)} %select_n.76), kind=kOutput, calls=%fused_computation.26 | convolution fusion | flops 4812963840 | bytes 17113092 | tf_op jit(solution)/shard_map/dot_general | solution.py:205
  233.2 7.2 %collective-permute-done = bf16[2176,2560]{1,0:T(8,128)(2,1)} collective-permute-done((bf16[2176,2560]{1,0:T(8,128)(2,1)}, bf16[2176,2560]{1,0:T(8,128)(2,1)}, u32[]{:S(2)}, u32[]{:S(2)}) %collective-permute-start) | collective-permute-done | bytes 11141152 | tf_op jit(solution)/shard_map/ppermute | solution.py:200
  240.5 8.5 %convolution_add_fusion = f32[2176,432]{0,1:T(8,128)S(1)} fusion(f32[2176,432]{0,1:T(8,128)S(1)} %fusion.12, bf16[2176,2560]{1,0:T(8,128)(2,1)} %collective-permute-done, bf16[5120,432]{0,1:T(8,128)(2,1)S(1)} %constant_dynamic-update-slice_fusion, s32[]{:T(128)S(6)} %select_n.77), kind=kOutput, calls=%fused_computation.10 | convolution fusion | flops 4813903872 | bytes 20873220 | tf_op jit(solution)/shard_map/dot_general | solution.py:205
  249.0 1.6 fusion.16
  250.6 45.7 %all-gather.12.cloned.1.call-done = bf16[2176,1728]{0,1:T(8,128)(2,1)} async-done(((bf16[2176,216]{0,1:T(8,128)(2,1)}), bf16[2176,1728]{0,1:T(8,128)(2,1)}) %all-gather.12.cloned.1.call-update) | async-done | bytes 7520272 | tf_op jit(solution)/shard_map/all_gather | solution.py:214
  296.3 9.0 %convolution_convert_fusion.1 = bf16[2176,640]{1,0:T(8,128)(2,1)S(1)} fusion(bf16[2176,1728]{0,1:T(8,128)(2,1)} %all-gather.12.cloned.1.call-done, bf16[1728,640]{1,0:T(8,128)(2,1)S(1)} %copy-done.23), kind=kOutput, calls=%fused_computation.9 | convolution fusion | flops 4814356480 | bytes 12517376 | tf_op jit(solution)/shard_map/dot_general | solution.py:215
  305.4 43.0 %all_to_all.29 = bf16[16,136,640]{2,1,0:T(8,128)(2,1)S(1)} all-to-all(bf16[16,136,640]{2,1,0:T(8,128)(2,1)S(1)} %bitcast.178), channel_id=1, replica_groups=mesh['req'=16,'mlp'=8] {'req'}, dimensions={0} | all-to-all | bytes 5570560 | tf_op jit(solution)/shard_map/all_to_all | solution.py:216
  349.3 0.7 add_convert_fusion
  (97 shorter events, 6.8 us)
Async XLA Ops:
  6.5 19.4 %copy-start = (bf16[3,4096,128]{2,1,0:T(8,128)(2,1)S(1)}, bf16[3,4096,128]{2,1,0:T(8,128)(2,1)}, u32[]{:S(2)}) copy-start(bf16[3,4096,128]{2,1,0:T(8,128)(2,1)} %param.21) | copy-start | bytes 9437188
  6.5 12.7 %copy-start.11 = (bf16[136,640]{1,0:T(8,128)(2,1)S(1)}, bf16[136,640]{1,0:T(8,128)(2,1)}, u32[]{:S(2)}) copy-start(bf16[136,640]{1,0:T(8,128)(2,1)} %param.18) | copy-start | bytes 522244
  6.5 12.7 %copy-start.24 = (s32[3]{0:T(128)S(1)}, s32[3]{0:T(128)}, u32[]{:S(2)}) copy-start(s32[3]{0:T(128)} %param.26) | copy-start | bytes 40
  6.5 13.3 %copy-start.2 = (s32[4]{0:T(128)S(1)}, s32[4]{0:T(128)}, u32[]{:S(2)}) copy-start(s32[4]{0:T(128)} %param.27) | copy-start | bytes 52
  6.5 17.8 %copy-start.22 = (s32[3]{0:T(128)S(1)}, s32[3]{0:T(128)}, u32[]{:S(2)}) copy-start(s32[3]{0:T(128)} %param.25) | copy-start | bytes 40
  6.5 57.4 %all-gather.14.cloned.1.call-start = ((), (), s32[]{:S(2)}) async-start(), calls=%async_computation.6 | async-start | bytes 2785280 | tf_op jit(solution)/shard_map/all_gather | solution.py:105
  10.3 28.6 %all-to-all-start = ((bf16[16,272,128]{2,1,0:T(8,128)(2,1)}), bf16[16,272,128]{2,1,0:T(8,128)(2,1)}, u32[]{:S(2)}, u32[]{:S(2)}) async-start(bf16[16,272,128]{2,1,0:T(8,128)(2,1)} %broadcast_in_dim.145), calls=%async_computation | async-start | bytes 2228224 | tf_op jit(solution)/shard_map/all_to_all | solution.py:108
  18.5 116.4 %all-gather.8.cloned.1.call-start = ((), (), s32[]{:S(2)}) async-start(), calls=%async_computation.3 | async-start | bytes 1566720 | tf_op jit(solution)/shard_map/all_gather | solution.py:189
  19.2 5.2 %copy-start.14 = (bf16[3,5,128]{2,1,0:T(8,128)(2,1)}, bf16[3,5,128]{2,1,0:T(8,128)(2,1)S(1)}, u32[]{:S(2)}) copy-start(bf16[3,5,128]{2,1,0:T(8,128)(2,1)S(1)} %reshape.382) | copy-start | bytes 11524
  25.9 2.2 copy-start.21
  28.2 13.6 %copy-start.5 = (bf16[133,5,128]{2,1,0:T(8,128)(2,1)S(1)}, bf16[133,5,128]{2,1,0:T(8,128)(2,1)}, u32[]{:S(2)}) copy-start(bf16[133,5,128]{2,1,0:T(8,128)(2,1)} %reshape.390) | copy-start | bytes 510724
  68.6 6.4 %copy-start.13 = (pred[3,1024]{1,0:T(4,128)(4,1)S(1)}, pred[3,1024]{1,0:T(4,128)(4,1)}, u32[]{:S(2)}) copy-start(pred[3,1024]{1,0:T(4,128)(4,1)} %iota_compare_fusion.2) | copy-start | bytes 9220
  68.6 6.4 %copy-start.15 = (bf16[3,5,128]{2,1,0:T(8,128)(2,1)S(1)}, bf16[3,5,128]{2,1,0:T(8,128)(2,1)}, u32[]{:S(2)}) copy-start(bf16[3,5,128]{2,1,0:T(8,128)(2,1)} %copy-done.14) | copy-start | bytes 11524
  68.6 8.0 %copy-start.16 = (f32[3,5]{1,0:T(4,128)S(1)}, f32[3,5]{1,0:T(4,128)}, u32[]{:S(2)}) copy-start(f32[3,5]{1,0:T(4,128)} %get-tuple-element.26) | copy-start | bytes 184
  68.6 8.0 %copy-start.19 = (f32[3,1,5]{2,1,0:T(1,128)S(1)}, f32[3,1,5]{2,1,0:T(1,128)}, u32[]{:S(2)}) copy-start(f32[3,1,5]{2,1,0:T(1,128)} %fusion.75) | copy-start | bytes 184
  68.6 12.8 %slice-start = ((s8[5918720]{0:T(1024)(128)(4,1)}), s8[1724416]{0:T(1024)(128)(4,1)S(1)}, s32[]{:S(2)}) async-start(s8[5918720]{0:T(1024)(128)(4,1)} %bitcast.166), calls=%async_computation.7 | async-start | bytes 3448832
  69.8 8.4 %copy-start.18 = (f32[3,128]{1,0:T(4,128)S(1)}, f32[3,128]{1,0:T(4,128)}, u32[]{:S(2)}) copy-start(f32[3,128]{1,0:T(4,128)} %slice_convert_fusion) | copy-start | bytes 4612
  75.0 5.7 %copy-start.6 = (bf16[133,5,128]{2,1,0:T(8,128)(2,1)S(1)}, bf16[133,5,128]{2,1,0:T(8,128)(2,1)}, u32[]{:S(2)}) copy-start(bf16[133,5,128]{2,1,0:T(8,128)(2,1)} %reshape.390) | copy-start | bytes 510724
  75.0 5.7 %copy-start.8 = (bf16[1,16,64,128]{3,2,0,1:T(8,128)(2,1)S(1)}, bf16[1,16,64,128]{3,2,0,1:T(8,128)(2,1)}, u32[]{:S(2)}) copy-start(bf16[1,16,64,128]{3,2,0,1:T(8,128)(2,1)} %slice.66) | copy-start | bytes 786436
  75.0 5.7 %copy-start.17 = (pred[1024]{0:T(1024)(128)(4,1)S(1)}, pred[1024]{0:T(1024)(128)(4,1)}, u32[]{:S(2)}) copy-start(pred[1024]{0:T(1024)(128)(4,1)} %iota_compare_fusion.3) | copy-start | bytes 3076
  76.8 4.7 %slice-start.1 = ((s8[5918720]{0:T(1024)(128)(4,1)}), s8[4194304]{0:T(1024)(128)(4,1)S(1)}, s32[]{:S(2)}) async-start(s8[5918720]{0:T(1024)(128)(4,1)} %bitcast.166), calls=%async_computation.8 | async-start | bytes 8388608
  82.9 1.0 copy-start.10
  83.8 1.0 copy-start.9
  83.8 2.5 slice-start.2
  84.9 2.3 slice-start.3
  88.6 24.1 %copy-start.12 = (bf16[136,640]{1,0:T(8,128)(2,1)S(1)}, bf16[136,640]{1,0:T(8,128)(2,1)}, u32[]{:S(2)}) copy-start(bf16[136,640]{1,0:T(8,128)(2,1)} %param.17) | copy-start | bytes 522244
  88.6 24.9 %copy-start.20 = (f32[640]{0:T(1024)S(1)}, f32[640]{0:T(1024)}, u32[]{:S(2)}) copy-start(f32[640]{0:T(1024)} %param.30) | copy-start | bytes 7684
  113.4 109.6 %all-gather.10.cloned.1.call-start = ((), (), s32[]{:S(2)}) async-start(), calls=%async_computation.4 | async-start | bytes 11837440 | tf_op jit(solution)/shard_map/all_gather | solution.py:198
  136.6 86.4 %copy-start.3 = (bf16[5120,216]{0,1:T(8,128)(2,1)S(1)}, bf16[5120,216]{0,1:T(8,128)(2,1)}, u32[]{:S(2)}) copy-start(bf16[5120,216]{0,1:T(8,128)(2,1)} %param.31) | copy-start | bytes 6635524
  139.5 156.8 %all-gather.12.cloned.1.call-start = ((), (), s32[]{:S(2)}) async-start(), calls=%async_computation.5 | async-start | bytes 8460288 | tf_op jit(solution)/shard_map/all_gather | solution.py:214
  223.0 17.4 %collective-permute-start = (bf16[2176,2560]{1,0:T(8,128)(2,1)}, bf16[2176,2560]{1,0:T(8,128)(2,1)}, u32[]{:S(2)}, u32[]{:S(2)}) collective-permute-start(bf16[2176,2560]{1,0:T(8,128)(2,1)} %all-gather.10.cloned.1.call-done), channel_id=1, source_target_pairs={{0,1},{1,0},{2,3},{3,2},{4,5},{5,4},{6,7},{7,6},{8,9},{9,8},{10,11... | collective-permute-start | bytes 33423368 | tf_op jit(solution)/shard_map/ppermute | solution.py:200
  223.0 1.6 copy-start.4
  249.0 47.3 %copy-start.23 = (bf16[1728,640]{1,0:T(8,128)(2,1)S(1)}, bf16[1728,640]{1,0:T(8,128)(2,1)}, u32[]{:S(2)}) copy-start(bf16[1728,640]{1,0:T(8,128)(2,1)} %param.33) | copy-start | bytes 6635524
  305.4 44.6 %copy-start.1 = (bf16[3,4096,128]{2,1,0:T(8,128)(2,1)S(1)}, bf16[3,4096,128]{2,1,0:T(8,128)(2,1)}, u32[]{:S(2)}) copy-start(bf16[3,4096,128]{2,1,0:T(8,128)(2,1)} %param.21) | copy-start | bytes 9437188
  348.4 0.9 copy-start.7
Sparse Core Ops, SparseCore 0:
  9.5 54.4 all-gather.13
  113.5 21.3 all-gather.7
  139.6 83.3 all-gather.9
  250.7 45.5 all-gather.11
where the time goes:
time: 357 us
  waiting for transfers between devices  174 us (49%)
  blocking collectives  79.7 us (22%)
  matrix products  40.9 us (11%)
  local copies, waits for them, and re-layouts  21.1 us (6%)
  other arithmetic  18.2 us (5%)
  between operations  14.2 us (4%)
  starting transfers between devices  8.37 us (2%)
    all_gather x1, waiting for transfers between devices, per_device(): near_rows = lax.all_gather(normed, 'req', axis=0, tiled=True)  83.5 us
    all_gather x1, waiting for transfers between devices, per_device(): hidden_block = lax.all_gather(hidden, 'mlp', axis=1, tiled=True)  45.7 us
    all_to_all x1, blocking collectives, per_device(): lax.all_to_all(down_partial.astype(jnp.bfloat16), 'req', 0, 0, tiled=True)  43 us
    all_to_all x1, blocking collectives, per_device(): lax.all_to_all(head_partial.astype(jnp.bfloat16), 'mlp', 1, 0, tiled=True)  23.8 us
    all_gather x1, waiting for transfers between devices, per_device(): context_gathered = lax.all_gather(context_pack, 'req', axis=0, tiled=False)  18.5 us
    unnamed x1, blocking collectives  12.9 us
    all_to_all x1, waiting for transfers between devices, per_device(): lax.all_to_all(new_copies.reshape(req_count * new_pack.shape[0], -1), 're...  10.5 us
    dot_general x1, matrix products, per_device(): jnp.dot(hidden_block, down_weight, preferred_element_type=jnp.float32)  9.03 us
  transfers between devices with their start and end apart: 6, of which 6 were waited for; matrix products, arithmetic and copies ran while one was open for 7% of the time, Pallas kernels for 0%

commit v1 on v0

--- a/solution.py
+++ b/solution.py
@@ -195,7 +195,9 @@
     normed = (own_half * lax.rsqrt(square_total / D + 1e-06)[:, None] * own_gain[None, :]).astype(
         jnp.bfloat16
     )
-    near_rows = lax.all_gather(normed, "req", axis=0, tiled=True)
+    near_rows = jnp.concatenate(
+        lax.all_to_all(jnp.stack([normed] * lax.axis_size("req")), "req", 0, 0), axis=0
+    )
     pairs = [(i, i ^ 1) for i in range(mlp_count)]
     far_rows = lax.ppermute(near_rows, "mlp", pairs)
 

time: 357 us -> 406 us (1.14)
  blocking collectives: 79.7 us -> 212 us
  waiting for transfers between devices: 174 us -> 87.6 us
    all_to_all x0 -> x1, blocking collectives: none -> 133 us  [per_device(): lax.all_to_all(jnp.stack([normed] * lax.axis_size('req')), 'req', 0, 0)]
    all_gather x1 -> x0, waiting for transfers between devices: 83.5 us -> none  [per_device(): near_rows = lax.all_gather(normed, 'req', axis=0, tiled=True)]
    another operation x4 -> x5, local copies, waits for them, and re-layouts: 2.11 us -> 6.9 us  [the longest x1 4.79 us: per_device(): jnp.stack([normed] * lax.axis_size('req'))]
  transfers between devices with their start and end apart: 6 -> 5, of which waited for: 6 -> 5; matrix products, arithmetic and copies ran while one was open for 7% -> 6% of each run, Pallas kernels for 0% -> 0%
where the time goes in v1:
time: 406 us; the launch traced here: 405 us
  blocking collectives  212 us (52%)
  waiting for transfers between devices  87.6 us (22%)
  matrix products  39.9 us (10%)
  local copies, waits for them, and re-layouts  23.7 us (6%)
  other arithmetic  19.1 us (5%)
  between operations  14.3 us (4%)
  starting transfers between devices  8.33 us (2%)
    all_to_all x1, blocking collectives, per_device(): lax.all_to_all(jnp.stack([normed] * lax.axis_size('req')), 'req', 0, 0)  133 us
    all_to_all x1, blocking collectives, per_device(): lax.all_to_all(down_partial.astype(jnp.bfloat16), 'req', 0, 0, tiled=True)  43 us
    all_gather x1, waiting for transfers between devices, per_device(): hidden_block = lax.all_gather(hidden, 'mlp', axis=1, tiled=True)  42.8 us
    all_to_all x1, blocking collectives, per_device(): lax.all_to_all(head_partial.astype(jnp.bfloat16), 'mlp', 1, 0, tiled=True)  23.8 us
    all_gather x1, waiting for transfers between devices, per_device(): context_gathered = lax.all_gather(context_pack, 'req', axis=0, tiled=False)  18.5 us
    unnamed x1, blocking collectives  12.9 us
    all_to_all x1, waiting for transfers between devices, per_device(): lax.all_to_all(new_copies.reshape(req_count * new_pack.shape[0], -1), 're...  10.5 us
    dot_general x1, matrix products, per_device(): jnp.dot(hidden_block, down_weight, preferred_element_type=jnp.float32)  9.03 us
  transfers between devices with their start and end apart: 5, of which 5 were waited for; matrix products, arithmetic and copies ran while one was open for 6% of the time, Pallas kernels for 0%

profile of v1, /device:TPU:0, one launch (start us, length us, event | category | flops | bytes accessed | tf_op | source)
XLA Modules:
  0.0 405.3 jit_solution(3939358673811223908)
XLA Ops:
  6.6 1.8 pad_maximum_fusion
  8.4 0.8 pad_maximum_fusion.1
  9.2 1.1 broadcast_in_dim.145
  10.3 8.2 %all-to-all-start = ((bf16[16,272,128]{2,1,0:T(8,128)(2,1)}), bf16[16,272,128]{2,1,0:T(8,128)(2,1)}, u32[]{:S(2)}, u32[]{:S(2)}) async-start(bf16[16,272,128]{2,1,0:T(8,128)(2,1)} %broadcast_in_dim.145), calls=%async_computation | async-start | bytes 2228224 | tf_op jit(solution)/shard_map/all_to_all | solution.py:108
  19.3 0.6 pad_clamp_fusion
  19.9 0.6 gather_fusion
  21.1 0.7 slice_bitcast_fusion
  21.8 1.2 slice_convert_fusion
  23.0 0.7 iota_compare_fusion.2
  23.6 0.6 fusion.75
  25.0 0.9 reshape.395
  25.9 2.3 fusion.91
  28.4 10.5 %all-to-all-done = bf16[16,272,128]{2,1,0:T(8,128)(2,1)} async-done(((bf16[16,272,128]{2,1,0:T(8,128)(2,1)}), bf16[16,272,128]{2,1,0:T(8,128)(2,1)}, u32[]{:S(2)}, u32[]{:S(2)}) %all-to-all-start) | async-done | bytes 1114144 | tf_op jit(solution)/shard_map/all_to_all | solution.py:108
  39.0 1.6 fusion.89
  40.5 1.0 reshape.445
  41.7 3.7 fusion.90
  45.5 18.5 %all-gather.11.cloned.1.call-done = bf16[10240,128]{1,0:T(8,128)(2,1)} async-done(((bf16[640,128]{1,0:T(8,128)(2,1)}), bf16[10240,128]{1,0:T(8,128)(2,1)}) %all-gather.11.cloned.1.call-update) | async-done | bytes 2621456 | tf_op jit(solution)/shard_map/all_gather | solution.py:105
  64.0 1.9 fusion.88
  65.9 0.7 slice.67
  66.6 1.2 copy.27
  67.8 0.7 slice.66
  68.5 1.3 copy.26
  69.8 0.8 gather_fusion.2
  70.6 2.1 gather_fusion.1
  74.0 2.5 fusion.45
  76.5 0.7 bitcast_reduce_fusion
  77.2 4.2 %fusion = f32[133,5]{0,1:T(8,128)S(1)} fusion(f32[133,1,5,2128]{3,0,2,1:T(8,128)} %get-tuple-element.25, f32[133,5]{0,1:T(8,128)S(1)} %get-tuple-element.12, pred[133,2128]{1,0:T(8,128)(4,1)S(1)} %iota_compare_fusion), kind=kLoop, calls=%fused_computation.7 | loop fusion | flops 4244695 | bytes 5948824 | tf_op jit(solution)/shard_map/reduce_sum | solution.py:24
  81.4 0.8 fusion.14
  82.4 0.8 fusion.34
  83.8 1.4 fusion.52
  85.9 1.3 convolution_convert_fusion
  87.4 23.8 %all_to_all.33 = bf16[136,8,640]{2,0,1:T(8,128)(2,1)S(1)} all-to-all(bf16[136,8,640]{2,0,1:T(8,128)(2,1)S(1)} %bitcast.175), channel_id=1, replica_groups=mesh['req'=16,'mlp'=8] {'mlp'}, dimensions={1} | all-to-all | bytes 2785280 | tf_op jit(solution)/shard_map/all_to_all | solution.py:185
  111.5 0.7 add_convert_fusion.1
  112.3 12.9 %all-gather.2 = f32[8,1,640]{2,1,0:T(1,128)S(1)} all-gather(f32[1,1,640]{2,1,0:T(1,128)S(1)} %reshape.438), channel_id=2, replica_groups=mesh['req'=16,'mlp'=8] {'mlp'}, dimensions={0}, use_global_device_ids=true | all-gather | bytes 23040 | tf_op args[13]
  125.3 8.4 %all-gather.7.cloned.1.call-done = bf16[136,5120]{1,0:T(8,128)(2,1)} async-done(((bf16[136,640]{1,0:T(8,128)(2,1)}), bf16[136,5120]{1,0:T(8,128)(2,1)}) %all-gather.7.cloned.1.call-update) | async-done | bytes 1392656 | tf_op jit(solution)/shard_map/all_gather | solution.py:189
  133.7 1.7 multiply_reduce_fusion
  135.4 1.6 convert_element_type.68
  137.2 4.8 %stack.2 = bf16[16,136,2560]{2,1,0:T(8,128)(2,1)} broadcast(bf16[136,2560]{1,0:T(8,128)(2,1)S(1)} %multiply_convert_fusion), dimensions={1,2} | broadcast | bytes 11837440 | tf_op jit(solution)/shard_map/stack | solution.py:199
  142.0 132.7 %all_to_all.34 = bf16[16,136,2560]{2,1,0:T(8,128)(2,1)} all-to-all(bf16[16,136,2560]{2,1,0:T(8,128)(2,1)} %stack.2), channel_id=1, replica_groups=mesh['req'=16,'mlp'=8] {'req'}, dimensions={0} | all-to-all | bytes 22282240 | tf_op jit(solution)/shard_map/all_to_all | solution.py:199
  274.8 1.5 copy-done.5
  276.5 8.4 %fusion.12 = f32[2176,432]{0,1:T(8,128)S(1)} fusion(bf16[2176,2560]{1,0:T(8,128)(2,1)} %bitcast.29, bf16[5120,432]{0,1:T(8,128)(2,1)S(1)} %constant_dynamic-update-slice_fusion, s32[]{:T(128)S(6)} %select_n.76), kind=kOutput, calls=%fused_computation.26 | convolution fusion | flops 4812963840 | bytes 17113092 | tf_op jit(solution)/shard_map/dot_general | solution.py:207
  284.9 7.2 %collective-permute-done = bf16[2176,2560]{1,0:T(8,128)(2,1)} collective-permute-done((bf16[2176,2560]{1,0:T(8,128)(2,1)}, bf16[2176,2560]{1,0:T(8,128)(2,1)}, u32[]{:S(2)}, u32[]{:S(2)}) %collective-permute-start) | collective-permute-done | bytes 11141152 | tf_op jit(solution)/shard_map/ppermute | solution.py:202
  292.1 8.5 %convolution_add_fusion = f32[2176,432]{0,1:T(8,128)S(1)} fusion(f32[2176,432]{0,1:T(8,128)S(1)} %fusion.12, bf16[2176,2560]{1,0:T(8,128)(2,1)} %collective-permute-done, bf16[5120,432]{0,1:T(8,128)(2,1)S(1)} %constant_dynamic-update-slice_fusion, s32[]{:T(128)S(6)} %select_n.77), kind=kOutput, calls=%fused_computation.10 | convolution fusion | flops 4813903872 | bytes 20873220 | tf_op jit(solution)/shard_map/dot_general | solution.py:207
  300.6 1.6 fusion.16
  302.3 42.8 %all-gather.9.cloned.1.call-done = bf16[2176,1728]{0,1:T(8,128)(2,1)} async-done(((bf16[2176,216]{0,1:T(8,128)(2,1)}), bf16[2176,1728]{0,1:T(8,128)(2,1)}) %all-gather.9.cloned.1.call-update) | async-done | bytes 7520272 | tf_op jit(solution)/shard_map/all_gather | solution.py:216
  345.1 9.0 %convolution_convert_fusion.1 = bf16[2176,640]{1,0:T(8,128)(2,1)S(1)} fusion(bf16[2176,1728]{0,1:T(8,128)(2,1)} %all-gather.9.cloned.1.call-done, bf16[1728,640]{1,0:T(8,128)(2,1)S(1)} %copy-done.24), kind=kOutput, calls=%fused_computation.9 | convolution fusion | flops 4814356480 | bytes 12517376 | tf_op jit(solution)/shard_map/dot_general | solution.py:217
  354.1 43.0 %all_to_all.35 = bf16[16,136,640]{2,1,0:T(8,128)(2,1)S(1)} all-to-all(bf16[16,136,640]{2,1,0:T(8,128)(2,1)S(1)} %bitcast.179), channel_id=1, replica_groups=mesh['req'=16,'mlp'=8] {'req'}, dimensions={0} | all-to-all | bytes 5570560 | tf_op jit(solution)/shard_map/all_to_all | solution.py:218
  398.0 0.7 add_convert_fusion
  (98 shorter events, 6.3 us)
Async XLA Ops:
  6.5 19.3 %copy-start = (bf16[3,4096,128]{2,1,0:T(8,128)(2,1)S(1)}, bf16[3,4096,128]{2,1,0:T(8,128)(2,1)}, u32[]{:S(2)}) copy-start(bf16[3,4096,128]{2,1,0:T(8,128)(2,1)} %param.21) | copy-start | bytes 9437188
  6.5 12.7 %copy-start.12 = (bf16[136,640]{1,0:T(8,128)(2,1)S(1)}, bf16[136,640]{1,0:T(8,128)(2,1)}, u32[]{:S(2)}) copy-start(bf16[136,640]{1,0:T(8,128)(2,1)} %param.18) | copy-start | bytes 522244
  6.5 12.7 %copy-start.25 = (s32[3]{0:T(128)S(1)}, s32[3]{0:T(128)}, u32[]{:S(2)}) copy-start(s32[3]{0:T(128)} %param.26) | copy-start | bytes 40
  6.5 13.3 %copy-start.2 = (s32[4]{0:T(128)S(1)}, s32[4]{0:T(128)}, u32[]{:S(2)}) copy-start(s32[4]{0:T(128)} %param.27) | copy-start | bytes 52
  6.5 17.7 %copy-start.23 = (s32[3]{0:T(128)S(1)}, s32[3]{0:T(128)}, u32[]{:S(2)}) copy-start(s32[3]{0:T(128)} %param.25) | copy-start | bytes 40
  6.5 57.4 %all-gather.11.cloned.1.call-start = ((), (), s32[]{:S(2)}) async-start(), calls=%async_computation.6 | async-start | bytes 2785280 | tf_op jit(solution)/shard_map/all_gather | solution.py:105
  10.3 28.6 %all-to-all-start = ((bf16[16,272,128]{2,1,0:T(8,128)(2,1)}), bf16[16,272,128]{2,1,0:T(8,128)(2,1)}, u32[]{:S(2)}, u32[]{:S(2)}) async-start(bf16[16,272,128]{2,1,0:T(8,128)(2,1)} %broadcast_in_dim.145), calls=%async_computation | async-start | bytes 2228224 | tf_op jit(solution)/shard_map/all_to_all | solution.py:108
  18.5 115.2 %all-gather.7.cloned.1.call-start = ((), (), s32[]{:S(2)}) async-start(), calls=%async_computation.4 | async-start | bytes 1566720 | tf_op jit(solution)/shard_map/all_gather | solution.py:189
  19.3 5.1 %copy-start.15 = (bf16[3,5,128]{2,1,0:T(8,128)(2,1)}, bf16[3,5,128]{2,1,0:T(8,128)(2,1)S(1)}, u32[]{:S(2)}) copy-start(bf16[3,5,128]{2,1,0:T(8,128)(2,1)S(1)} %reshape.387) | copy-start | bytes 11524
  25.9 2.3 copy-start.22
  28.2 13.6 %copy-start.6 = (bf16[133,5,128]{2,1,0:T(8,128)(2,1)S(1)}, bf16[133,5,128]{2,1,0:T(8,128)(2,1)}, u32[]{:S(2)}) copy-start(bf16[133,5,128]{2,1,0:T(8,128)(2,1)} %reshape.395) | copy-start | bytes 510724
  67.8 2.0 copy-start.3
  68.5 4.3 %copy-start.14 = (pred[3,1024]{1,0:T(4,128)(4,1)S(1)}, pred[3,1024]{1,0:T(4,128)(4,1)}, u32[]{:S(2)}) copy-start(pred[3,1024]{1,0:T(4,128)(4,1)} %iota_compare_fusion.2) | copy-start | bytes 9220
  68.5 4.3 %copy-start.16 = (bf16[3,5,128]{2,1,0:T(8,128)(2,1)S(1)}, bf16[3,5,128]{2,1,0:T(8,128)(2,1)}, u32[]{:S(2)}) copy-start(bf16[3,5,128]{2,1,0:T(8,128)(2,1)} %copy-done.15) | copy-start | bytes 11524
  68.5 4.7 %copy-start.17 = (f32[3,5]{1,0:T(4,128)S(1)}, f32[3,5]{1,0:T(4,128)}, u32[]{:S(2)}) copy-start(f32[3,5]{1,0:T(4,128)} %get-tuple-element.26) | copy-start | bytes 184
  68.5 4.7 %copy-start.20 = (f32[3,1,5]{2,1,0:T(1,128)S(1)}, f32[3,1,5]{2,1,0:T(1,128)}, u32[]{:S(2)}) copy-start(f32[3,1,5]{2,1,0:T(1,128)} %fusion.75) | copy-start | bytes 184
  69.8 4.2 %copy-start.19 = (f32[3,128]{1,0:T(4,128)S(1)}, f32[3,128]{1,0:T(4,128)}, u32[]{:S(2)}) copy-start(f32[3,128]{1,0:T(4,128)} %slice_convert_fusion) | copy-start | bytes 4612
  72.8 3.7 copy-start.7
  72.8 3.7 copy-start.9
  72.8 3.7 copy-start.18
  77.2 6.0 %slice-start = ((s8[5918720]{0:T(1024)(128)(4,1)}), s8[1724416]{0:T(1024)(128)(4,1)S(1)}, s32[]{:S(2)}) async-start(s8[5918720]{0:T(1024)(128)(4,1)} %bitcast.167), calls=%async_computation.7 | async-start | bytes 3448832
  81.4 1.0 copy-start.11
  81.4 2.3 slice-start.1
  81.4 2.4 copy-start.10
  82.4 3.0 slice-start.2
  83.8 2.1 slice-start.3
  87.4 24.1 %copy-start.13 = (bf16[136,640]{1,0:T(8,128)(2,1)S(1)}, bf16[136,640]{1,0:T(8,128)(2,1)}, u32[]{:S(2)}) copy-start(bf16[136,640]{1,0:T(8,128)(2,1)} %param.17) | copy-start | bytes 522244
  87.4 24.8 %copy-start.21 = (f32[640]{0:T(1024)S(1)}, f32[640]{0:T(1024)}, u32[]{:S(2)}) copy-start(f32[640]{0:T(1024)} %param.30) | copy-start | bytes 7684
  112.2 232.9 %all-gather.9.cloned.1.call-start = ((), (), s32[]{:S(2)}) async-start(), calls=%async_computation.5 | async-start | bytes 8460288 | tf_op jit(solution)/shard_map/all_gather | solution.py:216
  142.0 132.7 %copy-start.4 = (bf16[5120,216]{0,1:T(8,128)(2,1)S(1)}, bf16[5120,216]{0,1:T(8,128)(2,1)}, u32[]{:S(2)}) copy-start(bf16[5120,216]{0,1:T(8,128)(2,1)} %param.31) | copy-start | bytes 6635524
  274.7 17.4 %collective-permute-start = (bf16[2176,2560]{1,0:T(8,128)(2,1)}, bf16[2176,2560]{1,0:T(8,128)(2,1)}, u32[]{:S(2)}, u32[]{:S(2)}) collective-permute-start(bf16[2176,2560]{1,0:T(8,128)(2,1)} %bitcast.29), channel_id=1, source_target_pairs={{0,1},{1,0},{2,3},{3,2},{4,5},{5,4},{6,7},{7,6},{8,9},{9,8},{10,11... | collective-permute-start | bytes 33423368 | tf_op jit(solution)/shard_map/ppermute | solution.py:202
  274.7 1.6 copy-start.5
  300.6 44.5 %copy-start.24 = (bf16[1728,640]{1,0:T(8,128)(2,1)S(1)}, bf16[1728,640]{1,0:T(8,128)(2,1)}, u32[]{:S(2)}) copy-start(bf16[1728,640]{1,0:T(8,128)(2,1)} %param.33) | copy-start | bytes 6635524
  354.1 44.6 %copy-start.1 = (bf16[3,4096,128]{2,1,0:T(8,128)(2,1)S(1)}, bf16[3,4096,128]{2,1,0:T(8,128)(2,1)}, u32[]{:S(2)}) copy-start(bf16[3,4096,128]{2,1,0:T(8,128)(2,1)} %param.21) | copy-start | bytes 9437188
  397.1 0.9 copy-start.8
Sparse Core Ops, SparseCore 0:
  9.5 54.4 all-gather.10
  112.3 21.3 all-gather.6
  302.4 42.6 all-gather.8
